TPU v7x, 32 devices: a whole 2x2x4 slice. The times are simulated.
32 devices in a mesh: groups: 2 (over y), dp: 4 (over z), tensor: 2 (over x), layer: 2 (over core).
Axes of the slice: x: 2, y: 2, z: 4, core: 2. Of those that a mesh axis runs over, the one named last changes fastest.
Arguments:
- hidden_in: bfloat16 [2, 8, 512, 14336], P('layer', ('groups', 'dp'), None, 'tensor'), parts along dimension 1, may hold values from -6 to 6
- out_grad: bfloat16 [2, 8, 512, 4096], P('layer', ('groups', 'dp'), 'tensor'), parts along dimension 1, may hold values from -6 to 6
- proj_in: bfloat16 [2, 14336, 64], P('layer', 'tensor'), may hold values from -0.046875 to 0.046875
- proj_out: bfloat16 [2, 4096, 64], P('layer'), may hold values from -0.09375 to 0.09375
- query_grads: bfloat16 [2, 1024, 4096], P('layer', 'dp', 'tensor'), may hold values from -1.5 to 1.5
- lengths: int32 [8], P(('groups', 'dp')), parts along dimension 0, may hold values from 128 to 512, as said below
- query_decision: int32 [1024], P('dp'), may hold values from 0 to 1023
Outputs:
- influence: float32 [8, 1024], P(('groups', 'dp')), parts along dimension 0
There are 2 independent parts, one for each index of `groups`. A program takes and returns all parts, laid end to end along the dimension named above; an argument that names none is the same for every part. Nothing has to cross between parts.
Inputs may be any that keep to these rules, and one draw needn't show every extreme that they name: `lengths`: in each part one transcript has all 512 tokens live and another has exactly 128.
All inputs are finite; a program needn't handle non-finite values.
Results may differ from a plain program's by a relative error of at most 0.004.
Values may be sent and summed in bfloat16 or wider, within the bound.
No kernel may reach another device: no remote copies, remote signals or barrier semaphores. Data moves between devices by JAX's collectives and lax.ppermute only.
A program may use at most 64 MiB of HBM per device.

v0:
```python
import jax
import jax.numpy as jnp
from jax import lax
from jax.sharding import PartitionSpec as P

DECISIONS = 1024


def decision_table(decisions):
    return (decisions[:, None] == jnp.arange(DECISIONS, dtype=jnp.int32)[None, :]).astype(
        jnp.float32
    )


def body(hidden_in, out_grad, proj_in, proj_out, query_grads, lengths, query_decision):
    hidden_rows = hidden_in[0]
    grad_rows = out_grad[0]
    side_hidden = proj_in[0]
    side_width = proj_out[0]
    query_rows = query_grads[0]
    ex_count = hidden_rows.shape[0]
    seq_shard = grad_rows.shape[1]
    first_pos = lax.axis_index("tensor") * seq_shard
    positions = first_pos + jnp.arange(seq_shard, dtype=jnp.int32)
    live_tokens = (positions[None, :] < lengths[:, None]).astype(jnp.float32)
    right = jnp.einsum("etd,dp->etp", grad_rows, side_width, preferred_element_type=jnp.float32)
    right = (right * live_tokens[:, :, None]).astype(jnp.bfloat16)
    left = jnp.einsum("etf,fp->etp", hidden_rows, side_hidden, preferred_element_type=jnp.float32)
    left_own = lax.psum_scatter(left, "tensor", scatter_dimension=1, tiled=True)
    partial_value = jnp.einsum(
        "etp,etq->epq", left_own, right.astype(jnp.float32), precision=lax.Precision.HIGHEST
    )
    partial_value = partial_value / lengths.astype(jnp.float32)[:, None, None]
    grad_part = lax.psum_scatter(partial_value, "tensor", scatter_dimension=1, tiled=True)
    grad_flat = grad_part.reshape(ex_count, -1).astype(jnp.bfloat16)
    block_rows = lax.all_gather(query_rows, "dp", axis=0, tiled=True)
    block_decisions = lax.all_gather(query_decision, "dp", axis=0, tiled=True)
    scores = jnp.einsum("ek,qk->eq", grad_flat, block_rows, preferred_element_type=jnp.float32)
    partial_dec = jnp.dot(scores, decision_table(block_decisions), precision=lax.Precision.HIGHEST)
    result = lax.psum(partial_dec, ("tensor", "layer"))
    return result


def solution(mesh):
    in_specs = (
        P("layer", ("groups", "dp"), None, "tensor"),
        P("layer", ("groups", "dp"), "tensor", None),
        P("layer", "tensor", None),
        P("layer", None, None),
        P("layer", "dp", "tensor"),
        P(("groups", "dp")),
        P("dp"),
    )
    out_specs = P(("groups", "dp"), None)
    return jax.shard_map(body, mesh=mesh, in_specs=in_specs, out_specs=out_specs, check_vma=False)
```

profile of v0, /device:TPU:0, one launch (start us, length us, event | category | flops | bytes accessed | tf_op | source)
XLA Modules:
  0.0 130.6 jit_solution(11717772726066423702)
XLA Ops:
  7.4 0.0 copy-start
  7.4 0.0 copy-start.2
  7.4 0.0 copy-start.1
  7.4 0.0 reduce-scatter.3.cloned.1.call-start
  7.4 6.4 %fusion.11 = f32[1,512,64]{1,2,0:T(8,128)} fusion(bf16[1,1,512,7168]{3,2,1,0:T(8,128)(2,1)} %param.7, bf16[1,7168,64]{1,2,0:T(8,128)(2,1)} %param.9), kind=kOutput, calls=%fused_computation.10 | convolution fusion | flops 469762048 | bytes 8388608 | tf_op jit(solution)/shard_map/etf,fp->etp/dot_general | solution.py:28
  13.8 0.0 reduce-scatter.3.cloned.1.call-update
  13.8 0.0 reduce-scatter.5.cloned.1.call-start
  14.5 0.0 copy-done
  14.5 0.0 copy-done.2
  14.6 0.7 fusion.14
  15.2 11.8 %reduce-scatter.3.cloned.1.call-done = f32[1,256,64]{1,2,0:T(8,128)} async-done(((f32[1,512,64]{1,2,0:T(8,128)}), f32[1,256,64]{1,2,0:T(8,128)}) %reduce-scatter.3.cloned.1.call-update) | async-done | bytes 65552 | tf_op jit(solution)/shard_map/reduce_scatter | solution.py:29
  27.1 1.6 %fusion.17 = f32[1,64,64]{2,1,0:T(8,128)} fusion(bf16[256,64]{1,0:T(8,128)(2,1)S(1)} %fusion.14, f32[1,256,64]{1,2,0:T(8,128)} %reduce-scatter.3.cloned.1.call-done, f32[]{:T(128)} %bitcast.7), kind=kOutput, calls=%fused_computation.13 | convolution fusion | flops 12587008 | bytes 114692 | tf_op jit(solution)/shard_map/etp,etq->epq/dot_general | solution.py:30
  28.7 0.0 reduce-scatter.5.cloned.1.call-update
  28.7 0.0 all-gather.4.cloned.1.call-start
  28.7 0.5 all-gather.4.cloned.1.call-update
  29.3 0.0 copy-done.1
  29.3 10.9 %all-gather.1 = s32[4,1,256]{2,1,0:T(1,128)S(1)} all-gather(s32[1,1,256]{2,1,0:T(1,128)S(1)} %bitcast.43), channel_id=1, replica_groups=mesh['groups'=2,'dp'=4,'tensor'=2,'layer'=2] {'dp'}, dimensions={0}, use_global_device_ids=true | all-gather | bytes 5120 | tf_op jit(solution)/shard_map/all_gather | solution.py:37
  40.2 0.0 reduce-scatter.5.cloned.1.call-done
  40.2 0.7 convert_element_type.30
  40.9 0.1 reshape.54
  41.0 70.4 %all-gather.4.cloned.1.call-done = bf16[1,1024,2048]{2,1,0:T(8,128)(2,1)} async-done(((bf16[1,256,2048]{2,1,0:T(8,128)(2,1)}), bf16[1,1024,2048]{2,1,0:T(8,128)(2,1)}) %all-gather.4.cloned.1.call-update) | async-done | bytes 4194320 | tf_op jit(solution)/shard_map/all_gather | solution.py:36
  111.4 3.4 %fusion.18 = f32[1024,1]{0,1:T(1,128)S(1)} fusion(bf16[2048,1]{0,1:T(2,128)(2,1)S(1)} %reshape.54, bf16[1,1024,2048]{2,1,0:T(8,128)(2,1)} %all-gather.4.cloned.1.call-done), kind=kOutput, calls=%fused_computation.14 | convolution fusion | flops 4194304 | bytes 4202496 | tf_op jit(solution)/shard_map/ek,qk->eq/dot_general | solution.py:38
  114.7 1.5 %fusion.4 = f32[1,1024]{1,0:T(1,128)S(1)} fusion(f32[1024,1]{0,1:T(1,128)S(1)} %fusion.18, s32[1024]{0:T(1024)S(1)} %bitcast.42), kind=kOutput, calls=%fused_computation.5 | convolution fusion | flops 13631488 | bytes 12288 | tf_op jit(solution)/shard_map/dot_general | solution.py:39
  116.2 7.0 %psum.7 = f32[1,1024]{1,0:T(1,128)} all-reduce(f32[1,1024]{1,0:T(1,128)S(1)} %fusion.4), channel_id=1, replica_groups=mesh['groups'=2,'dp'=4,'tensor'=2,'layer'=2] {'tensor','layer'}, use_global_device_ids=true, to_apply=%region_2.0 | all-reduce | flops 1024 | bytes 8192 | tf_op jit(solution)/shard_map/psum | solution.py:40
  (1 shorter events, 0.0 us)
Async XLA Ops:
  7.4 7.2 %copy-start = (bf16[1,1,256,4096]{3,2,1,0:T(8,128)(2,1)S(1)}, bf16[1,1,256,4096]{3,2,1,0:T(8,128)(2,1)}, u32[]{:S(2)}) copy-start(bf16[1,1,256,4096]{3,2,1,0:T(8,128)(2,1)} %param.8) | copy-start | bytes 6291460
  7.4 7.2 %copy-start.2 = (bf16[1,4096,64]{1,2,0:T(8,128)(2,1)S(1)}, bf16[1,4096,64]{1,2,0:T(8,128)(2,1)}, u32[]{:S(2)}) copy-start(bf16[1,4096,64]{1,2,0:T(8,128)(2,1)} %param.10) | copy-start | bytes 1572868
  7.4 21.9 %copy-start.1 = (s32[256]{0:T(256)S(1)}, s32[256]{0:T(256)}, u32[]{:S(2)}) copy-start(s32[256]{0:T(256)} %param.13) | copy-start | bytes 3076
  7.4 19.7 %reduce-scatter.3.cloned.1.call-start = ((), (), s32[]{:S(2)}) async-start(), calls=%async_computation.2 | async-start | bytes 196608 | tf_op jit(solution)/shard_map/reduce_scatter | solution.py:29
  13.8 26.4 %reduce-scatter.5.cloned.1.call-start = ((), (), s32[]{:S(2)}) async-start(), calls=%async_computation.3 | async-start | bytes 49152 | tf_op jit(solution)/shard_map/reduce_scatter | solution.py:34
  28.7 82.7 %all-gather.4.cloned.1.call-start = ((), (), s32[]{:S(2)}) async-start(), calls=%async_computation.4 | async-start | bytes 5242880 | tf_op jit(solution)/shard_map/all_gather | solution.py:36
Sparse Core Ops, SparseCore 0:
  13.9 13.0 reduce-scatter.2
  29.2 9.9 reduce-scatter.4
Sparse Core Ops, SparseCore 1:
  30.7 80.6 all-gather.3
where the time goes:
time: 131 us
  waiting for transfers between devices  82.7 us (63%)
  blocking collectives  17.9 us (14%)
  between operations  15.5 us (12%)
  matrix products  13.5 us (10%)
    all_gather x1, waiting for transfers between devices, body(): block_rows = lax.all_gather(query_rows, 'dp', axis=0, tiled=True)  70.4 us
    reduce_scatter x1, waiting for transfers between devices, body(): left_own = lax.psum_scatter(left, 'tensor', scatter_dimension=1, tiled=True)  11.8 us
    all_gather x1, blocking collectives, body(): block_decisions = lax.all_gather(query_decision, 'dp', axis=0, tiled=True)  10.9 us
    psum x1, blocking collectives, body(): result = lax.psum(partial_dec, ('tensor', 'layer'))  6.99 us
    dot_general x1, matrix products, body(): jnp.einsum('etf,fp->etp', hidden_rows, side_hidden, preferred_element_typ...  6.41 us
    dot_general x1, matrix products, body(): jnp.einsum('ek,qk->eq', grad_flat, block_rows, preferred_element_type=jnp...  3.37 us
  transfers between devices with their start and end apart: 3, of which 2 were waited for; matrix products, arithmetic and copies ran while one was open for 1% of the time, Pallas kernels for 0%

commit v1 on v0

--- a/solution.py
+++ b/solution.py
@@ -2,6 +2,7 @@
 import jax.numpy as jnp
 from jax import lax
 from jax.sharding import PartitionSpec as P
+from jax.lax import all_gather
 
 DECISIONS = 1024
 
@@ -37,7 +38,7 @@
     block_decisions = lax.all_gather(query_decision, "dp", axis=0, tiled=True)
     scores = jnp.einsum("ek,qk->eq", grad_flat, block_rows, preferred_element_type=jnp.float32)
     partial_dec = jnp.dot(scores, decision_table(block_decisions), precision=lax.Precision.HIGHEST)
-    result = lax.psum(partial_dec, ("tensor", "layer"))
+    result = all_gather(partial_dec, ("tensor", "layer")).sum(axis=0)
     return result
 
 

time: 131 us -> 130 us (level)
  blocking collectives: 17.9 us -> 16.1 us
    psum x1 -> x0, blocking collectives: 6.99 us -> none  [body(): result = lax.psum(partial_dec, ('tensor', 'layer'))]
    all_gather x0 -> x1, blocking collectives: none -> 5.2 us  [body(): result = all_gather(partial_dec, ('tensor', 'layer')).sum(axis=0)]
where the time goes in v1:
time: 130 us; the launch traced here: 129 us
  waiting for transfers between devices  82.7 us (64%)
  blocking collectives  16.1 us (12%)
  between operations  15.5 us (12%)
  matrix products  13.6 us (10%)
  other arithmetic  1.34 us (1%)
    all_gather x1, waiting for transfers between devices, body(): block_rows = lax.all_gather(query_rows, 'dp', axis=0, tiled=True)  70.4 us
    reduce_scatter x1, waiting for transfers between devices, body(): left_own = lax.psum_scatter(left, 'tensor', scatter_dimension=1, tiled=True)  11.7 us
    all_gather x1, blocking collectives, body(): block_decisions = lax.all_gather(query_decision, 'dp', axis=0, tiled=True)  10.9 us
    dot_general x1, matrix products, body(): jnp.einsum('etf,fp->etp', hidden_rows, side_hidden, preferred_element_typ...  6.41 us
    all_gather x1, blocking collectives, body(): result = all_gather(partial_dec, ('tensor', 'layer')).sum(axis=0)  5.2 us
    dot_general x1, matrix products, body(): jnp.einsum('ek,qk->eq', grad_flat, block_rows, preferred_element_type=jnp...  3.37 us
  transfers between devices with their start and end apart: 3, of which 2 were waited for; matrix products, arithmetic and copies ran while one was open for 1% of the time, Pallas kernels for 0%

profile of v1, /device:TPU:0, one launch (start us, length us, event | category | flops | bytes accessed | tf_op | source)
XLA Modules:
  0.0 129.5 jit_solution(596049260678587090)
XLA Ops:
  7.4 0.0 copy-start
  7.4 0.0 copy-start.1
  7.4 0.0 copy-start.2
  7.4 0.0 reduce-scatter.3.cloned.1.call-start
  7.4 6.4 %fusion.8 = f32[1,512,64]{1,2,0:T(8,128)} fusion(bf16[1,1,512,7168]{3,2,1,0:T(8,128)(2,1)} %param.7, bf16[1,7168,64]{1,2,0:T(8,128)(2,1)} %param.9), kind=kOutput, calls=%fused_computation.9 | convolution fusion | flops 469762048 | bytes 8388608 | tf_op jit(solution)/shard_map/etf,fp->etp/dot_general | solution.py:29
  13.8 0.0 reduce-scatter.3.cloned.1.call-update
  13.8 0.0 reduce-scatter.5.cloned.1.call-start
  14.5 0.0 copy-done
  14.5 0.0 copy-done.1
  14.6 0.8 fusion.14
  15.3 11.7 %reduce-scatter.3.cloned.1.call-done = f32[1,256,64]{1,2,0:T(8,128)} async-done(((f32[1,512,64]{1,2,0:T(8,128)}), f32[1,256,64]{1,2,0:T(8,128)}) %reduce-scatter.3.cloned.1.call-update) | async-done | bytes 65552 | tf_op jit(solution)/shard_map/reduce_scatter | solution.py:30
  27.1 1.6 %fusion.17 = f32[1,64,64]{2,1,0:T(8,128)} fusion(bf16[256,64]{0,1:T(8,128)(2,1)S(1)} %fusion.14, f32[1,256,64]{1,2,0:T(8,128)} %reduce-scatter.3.cloned.1.call-done, f32[]{:T(128)} %bitcast.7), kind=kOutput, calls=%fused_computation.13 | convolution fusion | flops 12587008 | bytes 114692 | tf_op jit(solution)/shard_map/etp,etq->epq/dot_general | solution.py:31
  28.7 0.0 reduce-scatter.5.cloned.1.call-update
  28.7 0.0 all-gather.5.cloned.1.call-start
  28.7 0.5 all-gather.5.cloned.1.call-update
  29.3 0.0 copy-done.2
  29.3 10.9 %all-gather.2 = s32[4,1,256]{2,1,0:T(1,128)S(1)} all-gather(s32[1,1,256]{2,1,0:T(1,128)S(1)} %bitcast.45), channel_id=1, replica_groups=mesh['groups'=2,'dp'=4,'tensor'=2,'layer'=2] {'dp'}, dimensions={0}, use_global_device_ids=true | all-gather | bytes 5120 | tf_op jit(solution)/shard_map/all_gather | solution.py:38
  40.2 0.7 convert_element_type.30
  40.9 0.1 reshape.58
  41.0 70.4 %all-gather.5.cloned.1.call-done = bf16[1,1024,2048]{2,1,0:T(8,128)(2,1)} async-done(((bf16[1,256,2048]{2,1,0:T(8,128)(2,1)}), bf16[1,1024,2048]{2,1,0:T(8,128)(2,1)}) %all-gather.5.cloned.1.call-update) | async-done | bytes 4194320 | tf_op jit(solution)/shard_map/all_gather | solution.py:37
  111.4 3.4 %fusion.18 = f32[1024,1]{0,1:T(1,128)S(1)} fusion(bf16[2048,1]{0,1:T(2,128)(2,1)S(1)} %reshape.58, bf16[1,1024,2048]{2,1,0:T(8,128)(2,1)} %all-gather.5.cloned.1.call-done), kind=kOutput, calls=%fused_computation.14 | convolution fusion | flops 4194304 | bytes 4202496 | tf_op jit(solution)/shard_map/ek,qk->eq/dot_general | solution.py:39
  114.8 1.5 %fusion.4 = f32[1,1024]{1,0:T(1,128)S(1)} fusion(f32[1024,1]{0,1:T(1,128)S(1)} %fusion.18, s32[1024]{0:T(1024)S(1)} %bitcast.44), kind=kOutput, calls=%fused_computation.5 | convolution fusion | flops 13631488 | bytes 12288 | tf_op jit(solution)/shard_map/dot_general | solution.py:40
  116.2 5.2 %all-gather.1 = f32[4096]{0:T(1024)S(1)} all-gather(f32[1024]{0:T(1024)S(1)} %bitcast.43), channel_id=3, replica_groups=mesh['groups'=2,'dp'=4,'tensor'=2,'layer'=2] {'tensor','layer'}, dimensions={0}, use_global_device_ids=true | all-gather | bytes 20480 | tf_op jit(solution)/shard_map/all_gather | solution.py:41
  121.4 0.6 reduce.1
  (3 shorter events, 0.0 us)
Async XLA Ops:
  7.4 7.2 %copy-start = (bf16[1,1,256,4096]{3,2,1,0:T(8,128)(2,1)S(1)}, bf16[1,1,256,4096]{3,2,1,0:T(8,128)(2,1)}, u32[]{:S(2)}) copy-start(bf16[1,1,256,4096]{3,2,1,0:T(8,128)(2,1)} %param.8) | copy-start | bytes 6291460
  7.4 7.2 %copy-start.1 = (bf16[1,4096,64]{1,2,0:T(8,128)(2,1)S(1)}, bf16[1,4096,64]{1,2,0:T(8,128)(2,1)}, u32[]{:S(2)}) copy-start(bf16[1,4096,64]{1,2,0:T(8,128)(2,1)} %param.10) | copy-start | bytes 1572868
  7.4 21.9 %copy-start.2 = (s32[256]{0:T(256)S(1)}, s32[256]{0:T(256)}, u32[]{:S(2)}) copy-start(s32[256]{0:T(256)} %param.13) | copy-start | bytes 3076
  7.4 19.7 %reduce-scatter.3.cloned.1.call-start = ((), (), s32[]{:S(2)}) async-start(), calls=%async_computation.2 | async-start | bytes 196608 | tf_op jit(solution)/shard_map/reduce_scatter | solution.py:30
  13.8 26.4 %reduce-scatter.5.cloned.1.call-start = ((), (), s32[]{:S(2)}) async-start(), calls=%async_computation.3 | async-start | bytes 49152 | tf_op jit(solution)/shard_map/reduce_scatter | solution.py:35
  28.7 82.7 %all-gather.5.cloned.1.call-start = ((), (), s32[]{:S(2)}) async-start(), calls=%async_computation.4 | async-start | bytes 5242880 | tf_op jit(solution)/shard_map/all_gather | solution.py:37
Sparse Core Ops, SparseCore 0:
  13.9 13.0 reduce-scatter.2
  29.2 9.9 reduce-scatter.4
Sparse Core Ops, SparseCore 1:
  30.7 80.6 all-gather.4
